TPU v7x, 256 devices: a whole 4x4x8 slice. The times are simulated.
256 devices in a mesh: tm: 8 (over y_lo, x), stn: 32 (over y_hi, z, core).
Axes of the slice: x: 4, y: 4 (y_hi: 2, y_lo: 2; y = y_hi * 2 + y_lo), z: 8, core: 2. Of those that a mesh axis runs over, the one named last changes fastest.
Arguments:
- voltages: bfloat16 [1024, 524288], P('stn', 'tm'), may hold values from -6 to 6
- gains: float32 [2, 1024, 256], P(None, 'stn'), may hold values from -4 to 4
Outputs:
- visibility: float32 [256, 2, 1024, 1024], P(('tm', 'stn'))
All inputs are finite; a program needn't handle non-finite values.
Results may differ from a plain program's by a relative error of at most 0.0038.
Values may be sent and summed in bfloat16 or wider, within the bound.
No kernel may reach another device: no remote copies, remote signals or barrier semaphores. Data moves between devices by JAX's collectives and lax.ppermute only.
A program may use at most 128 MiB of HBM per device.

v0:
```python
import jax
import jax.numpy as jnp
from jax import lax
from jax.sharding import PartitionSpec as P

CHANNELS = 4096
BAND_LOW = 1024
TAPS = 8


def passed_along(x, axis, by):
    devices = lax.axis_size(axis)
    pairs = [(i, i + by) for i in range(devices) if 0 <= i + by < devices]
    return lax.ppermute(x, axis, pairs)


def window_table(chans):
    frame_len = 2 * chans
    total_len = TAPS * frame_len
    positions = jnp.arange(total_len, dtype=jnp.float32)
    centred = (positions - (total_len - 1) / 2.0) / frame_len
    taper = jnp.sin(jnp.pi * (positions + 0.5) / total_len)
    shaped = jnp.sinc(centred) * taper * taper
    shaped = shaped / jnp.sqrt(jnp.sum(shaped * shaped))
    return shaped.reshape(TAPS, frame_len)


def band_tables(frame_len, band):
    sample_index = jnp.arange(frame_len, dtype=jnp.int32)[:, None]
    channel_index = (BAND_LOW + jnp.arange(band, dtype=jnp.int32))[None, :]
    phase = (sample_index * channel_index % frame_len).astype(jnp.float32)
    angles = 2.0 * jnp.pi * phase / frame_len
    return (jnp.cos(angles), jnp.sin(angles))


def band_spectra(windowed, cos_table, sin_table):
    highest = lax.Precision.HIGHEST
    real_part = jnp.einsum("ifm,mk->kif", windowed, cos_table, precision=highest)
    imag_part = -jnp.einsum("ifm,mk->kif", windowed, sin_table, precision=highest)
    return (real_part, imag_part)


def apply_taps(window, extended, frames):
    windowed = jnp.zeros((extended.shape[0], frames, extended.shape[2]), jnp.float32)
    for tap_index in range(TAPS):
        windowed = windowed + window[tap_index] * extended[
            :, tap_index : tap_index + frames, :
        ].astype(jnp.float32)
    return windowed


def operands(turned):
    stacked = jnp.concatenate([turned[0], turned[1]], axis=-1)
    flipped = jnp.concatenate([turned[1], -turned[0]], axis=-1)
    return (stacked, flipped)


def cross_power(stacked, flipped, total_frames):
    vis_real = jnp.einsum("cif,cjf->cij", stacked, stacked, preferred_element_type=jnp.float32)
    vis_imag = jnp.einsum("cif,cjf->cij", flipped, stacked, preferred_element_type=jnp.float32)
    return jnp.stack([vis_real, vis_imag], axis=1) / total_frames


def on_device(voltages, gains):
    in_dev, length = voltages.shape
    band = gains.shape[2]
    frame_len = 2 * CHANNELS
    frames = length // frame_len
    n_time = lax.axis_size("tm")
    n_station = lax.axis_size("stn")
    per_device = band // (n_time * n_station)
    all_inputs = in_dev * n_station
    history = TAPS - 1
    window = window_table(CHANNELS)
    cos_table, sin_table = band_tables(frame_len, band)
    framed = voltages.reshape(in_dev, frames, frame_len)
    before = passed_along(framed[:, frames - history :, :], "tm", 1)
    extended = jnp.concatenate([before, framed], axis=1)
    windowed = apply_taps(window, extended, frames)
    raw_real, raw_imag = band_spectra(windowed, cos_table, sin_table)
    gain_real = jnp.transpose(gains[0])[:, :, None]
    gain_imag = jnp.transpose(gains[1])[:, :, None]
    spec_real = gain_real * raw_real - gain_imag * raw_imag
    spec_imag = gain_real * raw_imag + gain_imag * raw_real
    spectra = jnp.stack([spec_real, spec_imag]).astype(jnp.bfloat16)
    blocks = spectra.reshape(2, n_time, n_station, per_device, in_dev, frames)
    turned = lax.all_to_all(
        lax.all_to_all(blocks, "tm", split_axis=1, concat_axis=5, tiled=True),
        "stn",
        split_axis=2,
        concat_axis=4,
        tiled=True,
    )
    turned = turned.reshape(2, per_device, all_inputs, n_time * frames)
    stacked, flipped = operands(turned)
    return cross_power(stacked, flipped, float(n_time * frames))


def solution(mesh):
    in_specs = (P("stn", "tm"), P(None, "stn", None))
    out_specs = P(("tm", "stn"), None, None, None)
    return jax.shard_map(
        on_device, mesh=mesh, in_specs=in_specs, out_specs=out_specs, check_vma=False
    )
```

profile of v0, /device:TPU:1, one launch (start us, length us, event | category | flops | bytes accessed | tf_op | source)
XLA Modules:
  0.0 223.4 jit_solution(14158245446705456912)
XLA Ops:
  0.0 0.0 copy-start.1
  0.0 2.5 %copy.34 = bf16[4,8,8,8192]{3,2,0,1:T(8,128)(2,1)S(1)} copy(bf16[4,8,8,8192]{3,2,1,0:T(8,128)(2,1)} %bitcast.57) | data formatting | bytes 8388608 | tf_op jit(solution)/shard_map/reshape | solution.py:76
  2.5 2.1 slice.94
  4.6 5.7 %collective-permute-start = (bf16[32,7,8192]{2,0,1:T(8,128)(2,1)}, bf16[32,7,8192]{2,0,1:T(8,128)(2,1)}, u32[]{:S(2)}, u32[]{:S(2)}) collective-permute-start(bf16[32,7,8192]{2,0,1:T(8,128)(2,1)} %slice.94), channel_id=1, source_target_pairs={{0,32},{32,64},{64,96},{96,128},{128,160},{160,192},{192,224},{1,3... | collective-permute-start | bytes 11010056 | tf_op jit(solution)/shard_map/ppermute | solution.py:14
  10.3 1.9 multiply_reduce_fusion
  13.0 0.0 copy-start
  13.0 0.0 copy-done.1
  13.0 1.2 broadcast_divide_fusion
  14.3 72.5 %collective-permute-done = bf16[32,7,8192]{2,0,1:T(8,128)(2,1)} collective-permute-done((bf16[32,7,8192]{2,0,1:T(8,128)(2,1)}, bf16[32,7,8192]{2,0,1:T(8,128)(2,1)}, u32[]{:S(2)}, u32[]{:S(2)}) %collective-permute-start) | collective-permute-done | bytes 3670048 | tf_op jit(solution)/shard_map/ppermute | solution.py:14
  86.8 2.3 %constant_dynamic-update-slice_fusion.1 = bf16[32,15,8192]{2,0,1:T(8,128)(2,1)S(1)} fusion(bf16[32,7,8192]{2,0,1:T(8,128)(2,1)} %collective-permute-done), kind=kLoop, calls=%fused_computation.69 | loop fusion | bytes 7340032
  89.1 0.0 copy-done
  89.1 0.4 constant_dynamic-update-slice_fusion
  89.6 7.9 %multiply_add_fusion = f32[32,8,8192]{2,0,1:T(8,128)S(1)} fusion(bf16[32,15,8192]{2,0,1:T(8,128)(2,1)S(1)} %constant_dynamic-update-slice_fusion, f32[8192]{0:T(1024)S(1)} %get-tuple-element.10, f32[8192]{0:T(1024)S(1)} %get-tuple-element.11, f32[8192]{0:T(1024)S(1)} %get-tuple-element.12, f32[8192]{0:T(1024)S(1)} %get-tuple-element.13, ...), kind=kLoop, calls=%fused_computation.12 | loop fusion | flops 48234496 | bytes 42205184 | tf_op jit(solution)/shard_map/add | solution.py:46
  97.5 38.5 %fusion.5 = f32[256,32,8]{0,1,2:T(8,128)S(1)} fusion(f32[32,8,8192]{2,0,1:T(8,128)S(1)} %multiply_add_fusion, s32[256]{0:T(256)S(1)} %iota_add_fusion.2), kind=kOutput, calls=%fused_computation.9 | convolution fusion | flops 6471811072 | bytes 8651776 | tf_op jit(solution)/shard_map/ifm,mk->kif/dot_general | solution.py:38
  136.0 38.8 %subtract_convert_fusion = (bf16[256,32,8]{0,1,2:T(8,128)(2,1)S(1)}, bf16[256,32,8]{0,1,2:T(8,128)(2,1)S(1)}) fusion(f32[256,32,8]{0,1,2:T(8,128)S(1)} %fusion.5, f32[256,32]{0,1:T(8,128)S(1)} %get-tuple-element.18, f32[256,32]{0,1:T(8,128)S(1)} %get-tuple-element.17, f32[32,8,8192]{2,0,1:T(8,128)S(1)} %multiply_add_fusion, s32[256]{0:T(256)S(1)} %iota_add_fusion.2), kind=kOutput, calls=%fused_computation.63 | convolution fusion | flops 6472400896 | bytes 8979456 | tf_op jit(solution)/shard_map/ifm,mk->kif/dot_general | solution.py:39
  174.8 0.3 copy.25
  175.1 0.3 copy.26
  175.4 0.2 fusion.57
  175.6 1.0 reshape.144
  176.6 12.0 %all_to_all.27 = bf16[8,2,8192]{2,1,0:T(2,128)(2,1)S(1)} all-to-all(bf16[8,2,8192]{2,1,0:T(2,128)(2,1)S(1)} %reshape.144), channel_id=1, replica_groups=mesh['tm'=8,'stn'=32] {'tm'}, dimensions={0} | all-to-all | bytes 524288 | tf_op jit(solution)/shard_map/all_to_all | solution.py:88
  188.5 0.5 reshape.145
  189.0 0.3 copy_bitcast_fusion.1
  189.3 0.4 copy.24
  189.7 0.4 reshape.146
  190.1 26.8 %all_to_all.28 = bf16[32,2,2048]{2,1,0:T(2,128)(2,1)S(1)} all-to-all(bf16[32,2,2048]{2,1,0:T(2,128)(2,1)S(1)} %reshape.146), channel_id=1, replica_groups=mesh['tm'=8,'stn'=32] {'stn'}, dimensions={0} | all-to-all | bytes 524288 | tf_op jit(solution)/shard_map/all_to_all | solution.py:87
  216.9 0.4 reshape.147
  217.3 0.1 neg.22
  217.3 0.8 convolution_bitcast_fusion.1
  218.2 0.8 convolution_bitcast_fusion
  219.0 4.4 %maximum_multiply_fusion = f32[1,2,1024,1024]{3,2,1,0:T(8,128)} fusion(f32[1,1,1024,1024]{3,2,1,0:T(8,128)S(1)} %convolution_bitcast_fusion, f32[1,1,1024,1024]{3,2,1,0:T(8,128)S(1)} %convolution_bitcast_fusion.1), kind=kLoop, calls=%fused_computation.6 | loop fusion | flops 4194304 | bytes 16777216 | tf_op jit(solution)/shard_map/div | solution.py:61
  (4 shorter events, 0.1 us)
Async XLA Ops:
  0.0 13.0 %copy-start.1 = (f32[2,32,256]{2,1,0:T(8,128)S(1)}, f32[2,32,256]{2,1,0:T(8,128)}, u32[]{:S(2)}) copy-start(f32[2,32,256]{2,1,0:T(8,128)} %param.3) | copy-start | bytes 196612
  4.6 82.2 %collective-permute-start = (bf16[32,7,8192]{2,0,1:T(8,128)(2,1)}, bf16[32,7,8192]{2,0,1:T(8,128)(2,1)}, u32[]{:S(2)}, u32[]{:S(2)}) collective-permute-start(bf16[32,7,8192]{2,0,1:T(8,128)(2,1)} %slice.94), channel_id=1, source_target_pairs={{0,32},{32,64},{64,96},{96,128},{128,160},{160,192},{192,224},{1,3... | collective-permute-start | bytes 11010056 | tf_op jit(solution)/shard_map/ppermute | solution.py:14
  13.0 76.1 %copy-start = (bf16[32,65536]{1,0:T(8,128)(2,1)S(1)}, bf16[32,65536]{1,0:T(8,128)(2,1)}, u32[]{:S(2)}) copy-start(bf16[32,65536]{1,0:T(8,128)(2,1)} %param.2) | copy-start | bytes 12582916
where the time goes:
time: 224 us; the launch traced here: 223 us
  matrix products  78.9 us (35%)
  waiting for transfers between devices  72.5 us (32%)
  blocking collectives  38.7 us (17%)
  other arithmetic  15.7 us (7%)
  local copies, waits for them, and re-layouts  10.8 us (5%)
  starting transfers between devices  5.72 us (3%)
    ppermute x1, waiting for transfers between devices, passed_along(): return lax.ppermute(x, axis, pairs)  72.5 us
    dot_general x1, matrix products, band_spectra(): jnp.einsum('ifm,mk->kif', windowed, sin_table, precision=highest)  38.8 us
    dot_general x1, matrix products, band_spectra(): jnp.einsum('ifm,mk->kif', windowed, cos_table, precision=highest)  38.5 us
    all_to_all x1, blocking collectives, on_device(): lax.all_to_all(lax.all_to_all(blocks, 'tm', split_axis=1, concat_axis=5,...  26.8 us
    all_to_all x1, blocking collectives, on_device(): lax.all_to_all(blocks, 'tm', split_axis=1, concat_axis=5, tiled=True)  12 us
    add x1, other arithmetic, apply_taps(): windowed + window[tap_index] * extended[:, tap_index:tap_index + frames,...  7.9 us
    ppermute x1, starting transfers between devices, passed_along(): return lax.ppermute(x, axis, pairs)  5.72 us
  transfers between devices with their start and end apart: 1, of which 1 were waited for; matrix products, arithmetic and copies ran while one was open for 1% of the time, Pallas kernels for 0%

commit v1 on v0

--- a/solution.py
+++ b/solution.py
@@ -85,7 +85,10 @@
     spectra = jnp.stack([spec_real, spec_imag]).astype(jnp.bfloat16)
     blocks = spectra.reshape(2, n_time, n_station, per_device, in_dev, frames)
     turned = lax.all_to_all(
-        lax.all_to_all(blocks, "tm", split_axis=1, concat_axis=5, tiled=True),
+        jnp.concatenate(
+            lax.all_to_all(jnp.stack(jnp.split(blocks, lax.axis_size("tm"), axis=1)), "tm", 0, 0),
+            axis=5,
+        ),
         "stn",
         split_axis=2,
         concat_axis=4,

time: 224 us -> 224 us (level)
  no operation moved by 1% of the time
where the time goes in v1:
time: 224 us; the launch traced here: 223 us
  matrix products  78.9 us (35%)
  waiting for transfers between devices  72.5 us (32%)
  blocking collectives  38.7 us (17%)
  other arithmetic  15.9 us (7%)
  local copies, waits for them, and re-layouts  10.8 us (5%)
  starting transfers between devices  5.72 us (3%)
    ppermute x1, waiting for transfers between devices, passed_along(): return lax.ppermute(x, axis, pairs)  72.5 us
    dot_general x1, matrix products, band_spectra(): jnp.einsum('ifm,mk->kif', windowed, sin_table, precision=highest)  38.8 us
    dot_general x1, matrix products, band_spectra(): jnp.einsum('ifm,mk->kif', windowed, cos_table, precision=highest)  38.5 us
    all_to_all x1, blocking collectives, on_device(): lax.all_to_all(jnp.concatenate(lax.all_to_all(jnp.stack(jnp.split(blocks,...  26.8 us
    all_to_all x1, blocking collectives, on_device(): lax.all_to_all(jnp.stack(jnp.split(blocks, lax.axis_size('tm'), axis=1)),...  12 us
    add x1, other arithmetic, apply_taps(): windowed + window[tap_index] * extended[:, tap_index:tap_index + frames,...  7.9 us
    ppermute x1, starting transfers between devices, passed_along(): return lax.ppermute(x, axis, pairs)  5.72 us
  transfers between devices with their start and end apart: 1, of which 1 were waited for; matrix products, arithmetic and copies ran while one was open for 1% of the time, Pallas kernels for 0%

profile of v1, /device:TPU:1, one launch (start us, length us, event | category | flops | bytes accessed | tf_op | source)
XLA Modules:
  0.0 223.5 jit_solution(4223417254324137005)
XLA Ops:
  0.0 0.0 copy-start.1
  0.0 2.5 %copy.61 = bf16[4,8,8,8192]{3,2,0,1:T(8,128)(2,1)S(1)} copy(bf16[4,8,8,8192]{3,2,1,0:T(8,128)(2,1)} %bitcast.100) | data formatting | bytes 8388608 | tf_op jit(solution)/shard_map/reshape | solution.py:76
  2.5 2.1 slice.94
  4.6 5.7 %collective-permute-start = (bf16[32,7,8192]{2,0,1:T(8,128)(2,1)}, bf16[32,7,8192]{2,0,1:T(8,128)(2,1)}, u32[]{:S(2)}, u32[]{:S(2)}) collective-permute-start(bf16[32,7,8192]{2,0,1:T(8,128)(2,1)} %slice.94), channel_id=1, source_target_pairs={{0,32},{32,64},{64,96},{96,128},{128,160},{160,192},{192,224},{1,3... | collective-permute-start | bytes 11010056 | tf_op jit(solution)/shard_map/ppermute | solution.py:14
  10.3 1.9 multiply_reduce_fusion
  13.0 0.0 copy-start
  13.0 0.0 copy-done.1
  13.0 1.2 broadcast_divide_fusion
  14.3 72.5 %collective-permute-done = bf16[32,7,8192]{2,0,1:T(8,128)(2,1)} collective-permute-done((bf16[32,7,8192]{2,0,1:T(8,128)(2,1)}, bf16[32,7,8192]{2,0,1:T(8,128)(2,1)}, u32[]{:S(2)}, u32[]{:S(2)}) %collective-permute-start) | collective-permute-done | bytes 3670048 | tf_op jit(solution)/shard_map/ppermute | solution.py:14
  86.8 2.3 %constant_dynamic-update-slice_fusion.1 = bf16[32,15,8192]{2,0,1:T(8,128)(2,1)S(1)} fusion(bf16[32,7,8192]{2,0,1:T(8,128)(2,1)} %collective-permute-done), kind=kLoop, calls=%fused_computation.99 | loop fusion | bytes 7340032
  89.1 0.0 copy-done
  89.1 0.4 constant_dynamic-update-slice_fusion
  89.6 7.9 %multiply_add_fusion = f32[32,8,8192]{2,0,1:T(8,128)S(1)} fusion(bf16[32,15,8192]{2,0,1:T(8,128)(2,1)S(1)} %constant_dynamic-update-slice_fusion, f32[8192]{0:T(1024)S(1)} %get-tuple-element.10, f32[8192]{0:T(1024)S(1)} %get-tuple-element.11, f32[8192]{0:T(1024)S(1)} %get-tuple-element.12, f32[8192]{0:T(1024)S(1)} %get-tuple-element.13, ...), kind=kLoop, calls=%fused_computation.12 | loop fusion | flops 48234496 | bytes 42205184 | tf_op jit(solution)/shard_map/add | solution.py:46
  97.5 38.5 %fusion.5 = f32[256,32,8]{0,1,2:T(8,128)S(1)} fusion(f32[32,8,8192]{2,0,1:T(8,128)S(1)} %multiply_add_fusion, s32[256]{0:T(256)S(1)} %iota_add_fusion.2), kind=kOutput, calls=%fused_computation.9 | convolution fusion | flops 6471811072 | bytes 8651776 | tf_op jit(solution)/shard_map/ifm,mk->kif/dot_general | solution.py:38
  135.9 38.8 %subtract_convert_fusion = (bf16[256,32,8]{0,1,2:T(8,128)(2,1)S(1)}, bf16[256,32,8]{0,1,2:T(8,128)(2,1)S(1)}) fusion(f32[256,32,8]{0,1,2:T(8,128)S(1)} %fusion.5, f32[256,32]{0,1:T(8,128)S(1)} %get-tuple-element.18, f32[256,32]{0,1:T(8,128)S(1)} %get-tuple-element.17, f32[32,8,8192]{2,0,1:T(8,128)S(1)} %multiply_add_fusion, s32[256]{0:T(256)S(1)} %iota_add_fusion.2), kind=kOutput, calls=%fused_computation.76 | convolution fusion | flops 6472400896 | bytes 8979456 | tf_op jit(solution)/shard_map/ifm,mk->kif/dot_general | solution.py:39
  174.8 0.3 copy.52
  175.1 0.3 copy.53
  175.8 1.0 reshape.152
  176.7 12.0 %all_to_all.14 = bf16[8,2,8192]{2,1,0:T(2,128)(2,1)S(1)} all-to-all(bf16[8,2,8192]{2,1,0:T(2,128)(2,1)S(1)} %reshape.152), channel_id=1, replica_groups=mesh['tm'=8,'stn'=32] {'tm'}, dimensions={0} | all-to-all | bytes 524288 | tf_op jit(solution)/shard_map/all_to_all | solution.py:89
  188.7 0.5 reshape.153
  189.2 0.3 copy_bitcast_fusion.1
  189.5 0.4 copy.51
  189.9 0.4 reshape.154
  190.2 26.8 %all_to_all.15 = bf16[32,2,2048]{2,1,0:T(2,128)(2,1)S(1)} all-to-all(bf16[32,2,2048]{2,1,0:T(2,128)(2,1)S(1)} %reshape.154), channel_id=1, replica_groups=mesh['tm'=8,'stn'=32] {'stn'}, dimensions={0} | all-to-all | bytes 524288 | tf_op jit(solution)/shard_map/all_to_all | solution.py:87
  217.0 0.4 reshape.155
  217.4 0.1 neg.22
  217.5 0.8 convolution_bitcast_fusion.1
  218.3 0.8 convolution_bitcast_fusion
  219.1 4.4 %maximum_multiply_fusion = f32[1,2,1024,1024]{3,2,1,0:T(8,128)} fusion(f32[1,1,1024,1024]{3,2,1,0:T(8,128)S(1)} %convolution_bitcast_fusion, f32[1,1,1024,1024]{3,2,1,0:T(8,128)S(1)} %convolution_bitcast_fusion.1), kind=kLoop, calls=%fused_computation.6 | loop fusion | flops 4194304 | bytes 16777216 | tf_op jit(solution)/shard_map/div | solution.py:61
  (12 shorter events, 0.4 us)
Async XLA Ops:
  0.0 13.0 %copy-start.1 = (f32[2,32,256]{2,1,0:T(8,128)S(1)}, f32[2,32,256]{2,1,0:T(8,128)}, u32[]{:S(2)}) copy-start(f32[2,32,256]{2,1,0:T(8,128)} %param.3) | copy-start | bytes 196612
  4.6 82.2 %collective-permute-start = (bf16[32,7,8192]{2,0,1:T(8,128)(2,1)}, bf16[32,7,8192]{2,0,1:T(8,128)(2,1)}, u32[]{:S(2)}, u32[]{:S(2)}) collective-permute-start(bf16[32,7,8192]{2,0,1:T(8,128)(2,1)} %slice.94), channel_id=1, source_target_pairs={{0,32},{32,64},{64,96},{96,128},{128,160},{160,192},{192,224},{1,3... | collective-permute-start | bytes 11010056 | tf_op jit(solution)/shard_map/ppermute | solution.py:14
  13.0 76.1 %copy-start = (bf16[32,65536]{1,0:T(8,128)(2,1)S(1)}, bf16[32,65536]{1,0:T(8,128)(2,1)}, u32[]{:S(2)}) copy-start(bf16[32,65536]{1,0:T(8,128)(2,1)} %param.2) | copy-start | bytes 12582916
